TPU v7x, 512 devices: a whole 4x4x16 slice. The times are simulated.
512 devices in a mesh: seq: 32 (over y, z_hi, core), chan: 16 (over x, z_lo).
Axes of the slice: x: 4, y: 4, z: 16 (z_hi: 4, z_lo: 4; z = z_hi * 4 + z_lo), core: 2. Of those that a mesh axis runs over, the one named last changes fastest.
Arguments:
- streams: bfloat16 [5, 8192, 8192], P(None, 'seq', 'chan'), may hold values from -6 to 6
- short_filter: bfloat16 [7, 8192], P(None, 'chan'), may hold values from -2 to 2
- long_filter: bfloat16 [128, 8192], P(None, 'chan'), may hold values from -0.5 to 0.5
- edit_table: bfloat16 [64, 8, 8192], P('seq', None, 'chan'), may hold values from -0.25 to 0.25
- edit_bias: float32 [64, 4], replicated, may hold values from -8 to 8
- seq_tiles: int32 [4], replicated, may hold values from 1 to 32, 64 in all
- seq_tenant: int32 [4], replicated, may hold values from 0 to 63
Outputs:
- edited: bfloat16 [8192, 8192], P('seq', 'chan')
Inputs may be any that keep to these rules, and one draw needn't show every extreme that they name: `seq_tiles`: each sequence fills whole tiles; the sequences fill all 64 tiles in order and the longest has 32.
All inputs are finite; a program needn't handle non-finite values.
Results may differ from a plain program's by a relative error of at most 0.013.
Values may be sent and summed in bfloat16 or wider, within the bound.
No kernel may reach another device: no remote copies, remote signals or barrier semaphores. Data moves between devices by JAX's collectives and lax.ppermute only.
A program may use at most 64 MiB of HBM per device.

v0:
```python
import jax
import jax.numpy as jnp
from jax import lax
from jax.sharding import PartitionSpec as P

TILE_ROWS = 128
SEQS = 4


def from_behind(block, axis, distance):
    devices = range(lax.axis_size(axis))
    route = [(i - distance, i) for i in devices if i - distance in devices]
    return lax.ppermute(block, axis, route)


def depth_conv(window, taps_filter):
    width = window.shape[-1]
    kernel = taps_filter[::-1][:, None, :]
    return lax.conv_general_dilated(
        window,
        kernel,
        (1,),
        "VALID",
        dimension_numbers=("NWC", "WIO", "NWC"),
        feature_group_count=width,
        preferred_element_type=jnp.float32,
    )


def tiled_conv(field, border, starts, taps_filter):
    rows_here, width = field.shape
    reach = taps_filter.shape[0]
    tile_count = rows_here // TILE_ROWS
    tiles = field.reshape(tile_count, TILE_ROWS, width)
    trailing = tiles[:, TILE_ROWS - (reach - 1) :, :]
    earlier = jnp.concatenate([border[None], trailing[:-1]], axis=0)
    earlier = jnp.where(starts[:, None, None], jnp.zeros_like(earlier), earlier)
    window = jnp.concatenate([earlier, tiles], axis=1)
    return depth_conv(window, taps_filter).reshape(rows_here, width)


def on_device(streams, short_filter, long_filter, edit_table, edit_bias, seq_tiles, seq_tenant):
    rows_here = streams.shape[1]
    width = streams.shape[2]
    short_reach = short_filter.shape[0]
    long_reach = long_filter.shape[0]
    tile_count = rows_here // TILE_ROWS
    seq_ends = jnp.cumsum(seq_tiles)
    first_tile = lax.axis_index("seq") * tile_count
    tile_ids = first_tile + jnp.arange(tile_count, dtype=jnp.int32)
    seq_of = jnp.sum((seq_ends[None, :] <= tile_ids[:, None]).astype(jnp.int32), axis=1)
    starts = (tile_ids == 0) | jnp.any(seq_ends[None, :] == tile_ids[:, None], axis=1)
    first_gate = streams[0]
    first_key = streams[1]
    second_gate = streams[3]
    second_key = streams[4]
    gated = (first_key.astype(jnp.float32) * streams[2].astype(jnp.float32)).astype(jnp.bfloat16)
    short_border = from_behind(gated[rows_here - (short_reach - 1) :], "seq", 1)
    short_out = tiled_conv(gated, short_border, starts, short_filter)
    mixed = (first_gate.astype(jnp.float32) * short_out).astype(jnp.bfloat16)
    carried = (second_key.astype(jnp.float32) * mixed.astype(jnp.float32)).astype(jnp.bfloat16)
    long_border = from_behind(carried[rows_here - (long_reach - 1) :], "seq", 1)
    long_out = tiled_conv(carried, long_border, starts, long_filter)
    hidden = (second_gate.astype(jnp.float32) * long_out).astype(jnp.bfloat16)
    rows_per = edit_table.shape[1]
    rank = rows_per // 2
    all_rows = lax.all_gather(edit_table, "seq", axis=0, tiled=True)
    tenant_count = all_rows.shape[0]
    picker = (seq_tenant[:, None] == jnp.arange(tenant_count, dtype=jnp.int32)[None, :]).astype(
        jnp.bfloat16
    )
    chosen = jnp.dot(
        picker, all_rows.reshape(tenant_count, rows_per * width), preferred_element_type=jnp.float32
    )
    chosen = chosen.astype(jnp.bfloat16).reshape(SEQS, rows_per, width)
    tok_seq = jnp.repeat(seq_of, TILE_ROWS)
    seq_onehot = (tok_seq[:, None] == jnp.arange(SEQS, dtype=jnp.int32)[None, :]).astype(
        jnp.float32
    )
    projected = jnp.dot(
        hidden, chosen.reshape(SEQS * rows_per, width).T, preferred_element_type=jnp.float32
    )
    projected = projected.reshape(rows_here, SEQS, rows_per)
    selected = jnp.sum(projected * seq_onehot[:, :, None], axis=1)
    summed = lax.psum(selected, "chan")
    tenant_total = edit_bias.shape[0]
    bias_pick = (seq_tenant[:, None] == jnp.arange(tenant_total, dtype=jnp.int32)[None, :]).astype(
        jnp.float32
    )
    bias_seq = jnp.dot(bias_pick, edit_bias, precision=lax.Precision.HIGHEST)
    bias_tok = jnp.dot(seq_onehot, bias_seq, precision=lax.Precision.HIGHEST)
    coefficient = summed[:, rank:] - summed[:, :rank] + bias_tok
    spread = (seq_onehot[:, :, None] * coefficient[:, None, :]).reshape(rows_here, SEQS * rank)
    rows_r = chosen[:, :rank, :].reshape(SEQS * rank, width).astype(jnp.float32)
    change = jnp.dot(spread, rows_r, precision=lax.Precision.HIGHEST)
    return (hidden.astype(jnp.float32) + change).astype(jnp.bfloat16)


def solution(mesh):
    in_specs = (
        P(None, "seq", "chan"),
        P(None, "chan"),
        P(None, "chan"),
        P("seq", None, "chan"),
        P(),
        P(),
        P(),
    )
    out_specs = P("seq", "chan")
    return jax.shard_map(
        on_device, mesh=mesh, in_specs=in_specs, out_specs=out_specs, check_vma=False
    )
```

profile of v0, /device:TPU:8, one launch (start us, length us, event | category | flops | bytes accessed | tf_op | source)
XLA Modules:
  0.0 135.5 jit_solution(4230756904072077659)
XLA Ops:
  0.0 1.1 multiply_convert_fusion.3
  1.1 1.9 %collective-permute-start = (bf16[6,512]{1,0:T(8,128)(2,1)S(1)}, bf16[6,512]{1,0:T(8,128)(2,1)S(1)}, u32[]{:S(2)}, u32[]{:S(2)}) collective-permute-start(bf16[6,512]{1,0:T(8,128)(2,1)S(1)} %slice_bitcast_fusion), channel_id=1, source_target_pairs={{0,16},{16,32},{32,48},{48,64},{64,80},{80,96},{96,112},{112,128},... | collective-permute-start | bytes 18440 | tf_op jit(solution)/shard_map/ppermute | solution.py:13
  3.1 2.2 %slice_convert_fusion.2 = (f32[1,256,512]{2,1,0:T(8,128)S(1)}, f32[256,512]{1,0:T(8,128)S(1)}, f32[256,512]{1,0:T(8,128)}, f32[1,256,512]{2,1,0:T(8,128)S(1)}, f32[1,256,512]{2,1,0:T(8,128)S(1)}) fusion(bf16[5,256,512]{2,1,0:T(8,128)(2,1)} %param.7), kind=kLoop, calls=%fused_computation.30 | loop fusion | flops 393216 | bytes 3407872 | tf_op jit(solution)/shard_map/convert_element_type | solution.py:64
  5.3 0.2 reduce-window.8
  5.5 0.2 compare_reduce_fusion
  5.7 0.2 fusion.22
  6.0 56.8 %all_gather.3 = bf16[64,8,512]{2,1,0:T(8,128)(2,1)S(1)} all-gather(bf16[2,8,512]{2,1,0:T(8,128)(2,1)S(1)} %copy-done.4), channel_id=1, replica_groups=mesh['seq'=32,'chan'=16] {'seq'}, dimensions={0}, use_global_device_ids=true | all-gather | bytes 540672 | tf_op jit(solution)/shard_map/all_gather | solution.py:67
  62.9 0.2 convolution_convert_fusion
  63.3 1.3 rev.7
  64.8 0.2 copy.72
  65.1 0.2 pad.clone
  65.4 0.3 fusion.6
  65.7 0.3 convolution_select_fusion
  66.0 0.3 copy.67
  66.6 0.9 copy-done.1
  67.6 2.3 %collective-permute-start.1 = (bf16[127,512]{1,0:T(8,128)(2,1)S(1)}, bf16[127,512]{1,0:T(8,128)(2,1)S(1)}, u32[]{:S(2)}, u32[]{:S(2)}) collective-permute-start(bf16[127,512]{1,0:T(8,128)(2,1)S(1)} %fusion.9), channel_id=1, source_target_pairs={{0,16},{16,32},{32,48},{48,64},{64,80},{80,96},{96,112},{112,128},... | collective-permute-start | bytes 390152 | tf_op jit(solution)/shard_map/ppermute | solution.py:13
  69.9 0.2 fusion.20
  70.1 10.8 %collective-permute-done.1 = bf16[127,512]{1,0:T(8,128)(2,1)S(1)} collective-permute-done((bf16[127,512]{1,0:T(8,128)(2,1)S(1)}, bf16[127,512]{1,0:T(8,128)(2,1)S(1)}, u32[]{:S(2)}, u32[]{:S(2)}) %collective-permute-start.1) | collective-permute-done | bytes 130080 | tf_op jit(solution)/shard_map/ppermute | solution.py:13
  81.1 6.7 %fusion.4 = f32[2,128,512]{2,0,1:T(2,128)S(1)} fusion(bf16[2,255,512]{2,1,0:T(8,128)(2,1)S(1)} %pad_maximum_fusion, bf16[128,1,512]{2,0,1:T(8,128)(2,1)S(1)} %bitcast.63), kind=kOutput, calls=%fused_computation.16 | convolution fusion | flops 33554432 | bytes 1177600 | tf_op jit(solution)/shard_map/conv_general_dilated | solution.py:19
  88.0 0.2 fusion.2
  88.2 45.0 %psum.7 = f32[256,8]{0,1:T(8,128)S(1)} all-reduce(f32[256,8]{0,1:T(8,128)S(1)} %fusion.2), channel_id=1, replica_groups=mesh['seq'=32,'chan'=16] {'chan'}, use_global_device_ids=true, to_apply=%region_4.5 | all-reduce | flops 2048 | bytes 16384 | tf_op jit(solution)/shard_map/psum | solution.py:85
  133.1 1.0 fusion.3
  134.1 0.2 convolution_add_fusion
  134.3 1.2 fusion.1
  (37 shorter events, 1.4 us)
Async XLA Ops:
  0.0 69.9 %copy-start = (f32[64,4]{0,1:T(4,128)S(1)}, f32[64,4]{0,1:T(4,128)}, u32[]{:S(2)}) copy-start(f32[64,4]{0,1:T(4,128)} %param.11) | copy-start | bytes 3076
  1.1 63.6 %collective-permute-start = (bf16[6,512]{1,0:T(8,128)(2,1)S(1)}, bf16[6,512]{1,0:T(8,128)(2,1)S(1)}, u32[]{:S(2)}, u32[]{:S(2)}) collective-permute-start(bf16[6,512]{1,0:T(8,128)(2,1)S(1)} %slice_bitcast_fusion), channel_id=1, source_target_pairs={{0,16},{16,32},{32,48},{48,64},{64,80},{80,96},{96,112},{112,128},... | collective-permute-start | bytes 18440 | tf_op jit(solution)/shard_map/ppermute | solution.py:13
  3.1 2.3 %copy-start.7 = (s32[4]{0:T(128)S(1)}, s32[4]{0:T(128)}, u32[]{:S(2)}) copy-start(s32[4]{0:T(128)} %param.12) | copy-start | bytes 52
  3.1 2.9 %copy-start.4 = (bf16[2,8,512]{2,1,0:T(8,128)(2,1)S(1)}, bf16[2,8,512]{2,1,0:T(8,128)(2,1)}, u32[]{:S(2)}) copy-start(bf16[2,8,512]{2,1,0:T(8,128)(2,1)} %param.10) | copy-start | bytes 49156
  5.3 57.6 %copy-start.6 = (s32[4]{0:T(128)S(1)}, s32[4]{0:T(128)}, u32[]{:S(2)}) copy-start(s32[4]{0:T(128)} %param.13) | copy-start | bytes 52
  5.3 57.9 %copy-start.5 = (bf16[7,512]{1,0:T(8,128)(2,1)S(1)}, bf16[7,512]{1,0:T(8,128)(2,1)}, u32[]{:S(2)}) copy-start(bf16[7,512]{1,0:T(8,128)(2,1)} %param.8) | copy-start | bytes 21508
  5.3 58.0 %copy-start.2 = (bf16[128,512]{1,0:T(8,128)(2,1)S(1)}, bf16[128,512]{1,0:T(8,128)(2,1)}, u32[]{:S(2)}) copy-start(bf16[128,512]{1,0:T(8,128)(2,1)} %param.9) | copy-start | bytes 393220
  64.7 1.0 copy-start.8
  66.5 1.0 copy-start.1
  67.5 13.6 %copy-start.3 = (bf16[128,512]{1,0:T(8,128)(2,1)S(1)}, bf16[128,512]{1,0:T(8,128)(2,1)}, u32[]{:S(2)}) copy-start(bf16[128,512]{1,0:T(8,128)(2,1)} %rev.7) | copy-start | bytes 393220
  67.6 13.3 %collective-permute-start.1 = (bf16[127,512]{1,0:T(8,128)(2,1)S(1)}, bf16[127,512]{1,0:T(8,128)(2,1)S(1)}, u32[]{:S(2)}, u32[]{:S(2)}) collective-permute-start(bf16[127,512]{1,0:T(8,128)(2,1)S(1)} %fusion.9), channel_id=1, source_target_pairs={{0,16},{16,32},{32,48},{48,64},{64,80},{80,96},{96,112},{112,128},... | collective-permute-start | bytes 390152 | tf_op jit(solution)/shard_map/ppermute | solution.py:13
where the time goes:
time: 136 us
  blocking collectives  102 us (75%)
  waiting for transfers between devices  10.8 us (8%)
  matrix products  9 us (7%)
  other arithmetic  5.95 us (4%)
  starting transfers between devices  4.17 us (3%)
  local copies, waits for them, and re-layouts  3.59 us (3%)
    all_gather x1, blocking collectives, on_device(): all_rows = lax.all_gather(edit_table, 'seq', axis=0, tiled=True)  56.8 us
    psum x1, blocking collectives, on_device(): summed = lax.psum(selected, 'chan')  45 us
    ppermute x2, waiting for transfers between devices, from_behind(): return lax.ppermute(block, axis, route)  10.8 us
    conv_general_dilated x2, matrix products, depth_conv(): lax.conv_general_dilated(window, kernel, (1,), 'VALID', dimension_numbers...  7.03 us
    ppermute x2, starting transfers between devices, from_behind(): return lax.ppermute(block, axis, route)  4.17 us
    convert_element_type x3, other arithmetic, on_device(): hidden = (second_gate.astype(jnp.float32) * long_out).astype(jnp.bfloat16)  3.39 us
  transfers between devices with their start and end apart: 2, of which 1 were waited for; matrix products, arithmetic and copies ran while one was open for 4% of the time, Pallas kernels for 0%

commit v1 on v0

--- a/solution.py
+++ b/solution.py
@@ -1,3 +1,4 @@
+import functools
 import jax
 import jax.numpy as jnp
 from jax import lax
@@ -5,6 +6,15 @@
 
 TILE_ROWS = 128
 SEQS = 4
+
+
+def works_list(my_data, row_axis):
+    return jnp.concatenate(
+        lax.all_to_all(jnp.stack(lax.axis_size(row_axis) * [my_data], 0), row_axis, 0, 0), 0
+    )
+
+
+proceed_the_leaf = functools.partial(works_list, row_axis="seq")
 
 
 def from_behind(block, axis, distance):
@@ -64,7 +74,7 @@
     hidden = (second_gate.astype(jnp.float32) * long_out).astype(jnp.bfloat16)
     rows_per = edit_table.shape[1]
     rank = rows_per // 2
-    all_rows = lax.all_gather(edit_table, "seq", axis=0, tiled=True)
+    all_rows = proceed_the_leaf(edit_table)
     tenant_count = all_rows.shape[0]
     picker = (seq_tenant[:, None] == jnp.arange(tenant_count, dtype=jnp.int32)[None, :]).astype(
         jnp.bfloat16

time: 136 us -> 114 us (0.84)
  the two profiles are of different devices: /device:TPU:8 before, /device:TPU:24 now
where the time goes in v1:
time: 114 us
  blocking collectives  53.9 us (47%)
  starting transfers between devices  24.2 us (21%)
  waiting for transfers between devices  11.5 us (10%)
  matrix products  9.03 us (8%)
  local copies, waits for them, and re-layouts  7.86 us (7%)
  other arithmetic  6.82 us (6%)
    psum x1, blocking collectives, on_device(): summed = lax.psum(selected, 'chan')  53.9 us
    all_to_all x1, starting transfers between devices, works_list(): lax.all_to_all(jnp.stack(lax.axis_size(row_axis) * [my_data], 0), row_axi...  20.2 us
    ppermute x2, waiting for transfers between devices, from_behind(): return lax.ppermute(block, axis, route)  11.4 us
    conv_general_dilated x2, matrix products, depth_conv(): lax.conv_general_dilated(window, kernel, (1,), 'VALID', dimension_numbers...  7.06 us
    ppermute x2, starting transfers between devices, from_behind(): return lax.ppermute(block, axis, route)  3.94 us
    unnamed x33, local copies, waits for them, and re-layouts  2.71 us
    convert_element_type x3, other arithmetic, on_device(): hidden = (second_gate.astype(jnp.float32) * long_out).astype(jnp.bfloat16)  2.52 us
  transfers between devices with their start and end apart: 3, of which 1 were waited for; matrix products, arithmetic and copies ran while one was open for 16% of the time, Pallas kernels for 0%

profile of v1, /device:TPU:24, one launch (start us, length us, event | category | flops | bytes accessed | tf_op | source)
XLA Modules:
  0.0 113.5 jit_solution(4509380761886008372)
XLA Ops:
  0.0 1.2 %multiply_convert_fusion.3 = bf16[1,256,512]{2,1,0:T(8,128)(2,1)S(1)} fusion(bf16[5,256,512]{2,1,0:T(8,128)(2,1)} %param.7), kind=kLoop, calls=%fused_computation.15 | loop fusion | flops 524288 | bytes 786432 | tf_op jit(solution)/shard_map/convert_element_type | solution.py:67
  1.2 0.7 copy-done.4
  1.9 0.6 slice_bitcast_fusion
  2.5 1.9 %collective-permute-start = (bf16[6,512]{1,0:T(8,128)(2,1)}, bf16[6,512]{1,0:T(8,128)(2,1)}, u32[]{:S(2)}, u32[]{:S(2)}) collective-permute-start(bf16[6,512]{1,0:T(8,128)(2,1)} %slice_bitcast_fusion), channel_id=1, source_target_pairs={{0,16},{16,32},{32,48},{48,64},{64,80},{80,96},{96,112},{112,128},... | collective-permute-start | bytes 18440 | tf_op jit(solution)/shard_map/ppermute | solution.py:23
  4.4 1.6 %stack.2 = bf16[32,2,8,512]{3,2,1,0:T(8,128)(2,1)} broadcast(bf16[2,8,512]{2,1,0:T(8,128)(2,1)} %param.10), dimensions={1,2,3} | broadcast | bytes 540672 | tf_op jit(solution)/shard_map/stack | solution.py:13
  6.0 20.2 %all-to-all-start = ((bf16[32,2,8,512]{3,2,1,0:T(8,128)(2,1)}), bf16[32,2,8,512]{3,2,1,0:T(8,128)(2,1)S(1)}, u32[]{:S(2)}, u32[]{:S(2)}) async-start(bf16[32,2,8,512]{3,2,1,0:T(8,128)(2,1)} %stack.2), calls=%async_computation | async-start | bytes 1048576 | tf_op jit(solution)/shard_map/all_to_all | solution.py:13
  26.3 1.3 %slice_convert_fusion.2 = (f32[1,256,512]{2,1,0:T(8,128)S(1)}, f32[256,512]{1,0:T(8,128)}, f32[256,512]{1,0:T(8,128)}, f32[1,256,512]{2,1,0:T(8,128)S(1)}, f32[1,256,512]{2,1,0:T(8,128)S(1)}) fusion(bf16[5,256,512]{2,1,0:T(8,128)(2,1)S(1)} %copy-done.1), kind=kLoop, calls=%fused_computation.30 | loop fusion | flops 393216 | bytes 3407872 | tf_op jit(solution)/shard_map/convert_element_type | solution.py:74
  28.3 0.6 copy-done.10
  28.8 0.7 slice.59
  29.7 1.4 %rev.7 = bf16[128,512]{1,0:T(8,128)(2,1)} reverse(bf16[128,512]{1,0:T(8,128)(2,1)S(1)} %copy-done.5), dimensions={0} | reverse | bytes 262144 | tf_op jit(solution)/shard_map/rev | solution.py:28
  31.0 0.8 maximum_select_fusion.1
  31.8 1.0 pad_maximum_fusion.1
  33.1 0.2 pad.clone
  33.4 0.3 fusion.6
  33.7 0.3 convolution_select_fusion
  34.0 0.3 copy.54
  34.7 0.8 copy-done.2
  35.8 2.0 %collective-permute-start.1 = (bf16[127,512]{1,0:T(8,128)(2,1)S(1)}, bf16[127,512]{1,0:T(8,128)(2,1)S(1)}, u32[]{:S(2)}, u32[]{:S(2)}) collective-permute-start(bf16[127,512]{1,0:T(8,128)(2,1)S(1)} %fusion.9), channel_id=1, source_target_pairs={{0,16},{16,32},{32,48},{48,64},{64,80},{80,96},{96,112},{112,128},... | collective-permute-start | bytes 390152 | tf_op jit(solution)/shard_map/ppermute | solution.py:23
  38.0 11.4 %collective-permute-done.1 = bf16[127,512]{1,0:T(8,128)(2,1)S(1)} collective-permute-done((bf16[127,512]{1,0:T(8,128)(2,1)S(1)}, bf16[127,512]{1,0:T(8,128)(2,1)S(1)}, u32[]{:S(2)}, u32[]{:S(2)}) %collective-permute-start.1) | collective-permute-done | bytes 130080 | tf_op jit(solution)/shard_map/ppermute | solution.py:23
  49.7 6.7 %fusion.4 = f32[2,128,512]{2,0,1:T(2,128)S(1)} fusion(bf16[2,255,512]{2,1,0:T(8,128)(2,1)S(1)} %pad_maximum_fusion, bf16[128,1,512]{2,0,1:T(8,128)(2,1)S(1)} %bitcast.64), kind=kOutput, calls=%fused_computation.16 | convolution fusion | flops 33554432 | bytes 1177600 | tf_op jit(solution)/shard_map/conv_general_dilated | solution.py:29
  56.6 1.0 fusion.3
  57.8 0.2 convolution_convert_fusion
  58.3 53.9 %psum.7 = f32[256,8]{0,1:T(8,128)S(1)} all-reduce(f32[256,8]{0,1:T(8,128)S(1)} %fusion.2), channel_id=1, replica_groups=mesh['seq'=32,'chan'=16] {'chan'}, use_global_device_ids=true, to_apply=%region_4.5 | all-reduce | flops 2048 | bytes 16384 | tf_op jit(solution)/shard_map/psum | solution.py:95
  112.3 1.2 %fusion.1 = bf16[256,512]{1,0:T(8,128)(2,1)} fusion(bf16[256,512]{1,0:T(8,128)(2,1)S(1)} %fusion.3, bf16[4,8,512]{2,1,0:T(8,128)(2,1)S(1)} %bitcast.65, f32[256,4]{0,1:T(4,128)S(1)} %convolution_add_fusion, f32[256,4]{0,1:T(4,128)S(1)} %fusion.19), kind=kOutput, calls=%fused_computation.5 | convolution fusion | flops 25563136 | bytes 548864 | tf_op jit(solution)/shard_map/dot_general | solution.py:105
  (51 shorter events, 2.7 us)
Async XLA Ops:
  0.0 37.8 %copy-start = (f32[64,4]{0,1:T(4,128)S(1)}, f32[64,4]{0,1:T(4,128)}, u32[]{:S(2)}) copy-start(f32[64,4]{0,1:T(4,128)} %param.11) | copy-start | bytes 3076
  0.0 26.2 %copy-start.1 = (bf16[5,256,512]{2,1,0:T(8,128)(2,1)S(1)}, bf16[5,256,512]{2,1,0:T(8,128)(2,1)}, u32[]{:S(2)}) copy-start(bf16[5,256,512]{2,1,0:T(8,128)(2,1)} %param.7) | copy-start | bytes 3932164
  1.2 0.7 copy-start.4
  2.5 28.5 %collective-permute-start = (bf16[6,512]{1,0:T(8,128)(2,1)}, bf16[6,512]{1,0:T(8,128)(2,1)}, u32[]{:S(2)}, u32[]{:S(2)}) collective-permute-start(bf16[6,512]{1,0:T(8,128)(2,1)} %slice_bitcast_fusion), channel_id=1, source_target_pairs={{0,16},{16,32},{32,48},{48,64},{64,80},{80,96},{96,112},{112,128},... | collective-permute-start | bytes 18440 | tf_op jit(solution)/shard_map/ppermute | solution.py:23
  6.0 51.6 %all-to-all-start = ((bf16[32,2,8,512]{3,2,1,0:T(8,128)(2,1)}), bf16[32,2,8,512]{3,2,1,0:T(8,128)(2,1)S(1)}, u32[]{:S(2)}, u32[]{:S(2)}) async-start(bf16[32,2,8,512]{3,2,1,0:T(8,128)(2,1)} %stack.2), calls=%async_computation | async-start | bytes 1048576 | tf_op jit(solution)/shard_map/all_to_all | solution.py:13
  26.2 1.4 %copy-start.13 = (s32[4]{0:T(128)S(1)}, s32[4]{0:T(128)}, u32[]{:S(2)}) copy-start(s32[4]{0:T(128)} %param.12) | copy-start | bytes 52
  26.3 3.3 %copy-start.7 = (bf16[7,512]{1,0:T(8,128)(2,1)S(1)}, bf16[7,512]{1,0:T(8,128)(2,1)}, u32[]{:S(2)}) copy-start(bf16[7,512]{1,0:T(8,128)(2,1)} %param.8) | copy-start | bytes 21508
  26.3 3.4 %copy-start.5 = (bf16[128,512]{1,0:T(8,128)(2,1)S(1)}, bf16[128,512]{1,0:T(8,128)(2,1)}, u32[]{:S(2)}) copy-start(bf16[128,512]{1,0:T(8,128)(2,1)} %param.9) | copy-start | bytes 393220
  28.3 0.6 copy-start.10
  28.8 4.8 %copy-start.8 = (pred[2]{0:T(512)(128)(4,1)}, pred[2]{0:T(512)(128)(4,1)S(1)}, u32[]{:S(2)}) copy-start(pred[2]{0:T(512)(128)(4,1)S(1)} %compare_or_fusion) | copy-start | bytes 10
  31.0 2.7 %copy-start.14 = (pred[16,17]{0,1:T(8,128)(4,1)S(1)}, pred[16,17]{0,1:T(8,128)(4,1)}, u32[]{:S(2)}) copy-start(pred[16,17]{0,1:T(8,128)(4,1)} %constant.30) | copy-start | bytes 820
  34.5 1.0 copy-start.2
  34.5 1.2 %copy-start.3 = (f32[256,512]{1,0:T(8,128)S(1)}, f32[256,512]{1,0:T(8,128)}, u32[]{:S(2)}) copy-start(f32[256,512]{1,0:T(8,128)} %get-tuple-element.7) | copy-start | bytes 1572868
  34.5 3.3 %copy-start.12 = (s32[4]{0:T(128)S(1)}, s32[4]{0:T(128)}, u32[]{:S(2)}) copy-start(s32[4]{0:T(128)} %param.13) | copy-start | bytes 52
  34.5 15.0 %copy-start.9 = (pred[2]{0:T(512)(128)(4,1)S(1)}, pred[2]{0:T(512)(128)(4,1)}, u32[]{:S(2)}) copy-start(pred[2]{0:T(512)(128)(4,1)} %copy-done.8) | copy-start | bytes 10
  35.7 14.0 %copy-start.6 = (bf16[128,512]{1,0:T(8,128)(2,1)S(1)}, bf16[128,512]{1,0:T(8,128)(2,1)}, u32[]{:S(2)}) copy-start(bf16[128,512]{1,0:T(8,128)(2,1)} %rev.7) | copy-start | bytes 393220
  35.8 13.7 %collective-permute-start.1 = (bf16[127,512]{1,0:T(8,128)(2,1)S(1)}, bf16[127,512]{1,0:T(8,128)(2,1)S(1)}, u32[]{:S(2)}, u32[]{:S(2)}) collective-permute-start(bf16[127,512]{1,0:T(8,128)(2,1)S(1)} %fusion.9), channel_id=1, source_target_pairs={{0,16},{16,32},{32,48},{48,64},{64,80},{80,96},{96,112},{112,128},... | collective-permute-start | bytes 390152 | tf_op jit(solution)/shard_map/ppermute | solution.py:23
  56.6 55.6 %copy-start.11 = (s32[256]{0:T(256)S(1)}, s32[256]{0:T(256)}, u32[]{:S(2)}) copy-start(s32[256]{0:T(256)} %copy-done.10) | copy-start | bytes 3076
